TPU v7x, 32 devices: a whole 2x2x4 slice. The times are simulated.
32 devices in a mesh: mem: 4 (over z), tile: 8 (over y, x, core).
Axes of the slice: x: 2, y: 2, z: 4, core: 2. Of those that a mesh axis runs over, the one named last changes fastest.
Arguments:
- source_blocks: bfloat16 [1024, 8, 2, 256], P('tile', 'mem'), may hold values from -6 to 6
- send_blocks: int32 [8, 8, 24], P('tile'), may hold values from 0 to 127
- recv_slot: int32 [8, 8, 24], P('tile'), may hold values from 0 to 95
- recv_weight: float32 [8, 8, 24], P('tile'), may hold values from 0.25 to 2
- recv_count: int32 [8, 8], P('tile'), may hold values from 0 to 24, as said below
- regional: bfloat16 [8, 2, 512, 384], P('mem', None, 'tile'), may hold values from -6 to 6
- x_operator: bfloat16 [512, 512], P(('mem', 'tile'))
- y_operator: bfloat16 [384, 384], P(('mem', 'tile'))
Outputs:
- blended: bfloat16 [8, 2, 512, 384], P('mem', None, 'tile')
Inputs may be any that keep to these rules, and one draw needn't show every extreme that they name: `recv_count`: live entries of one pair of tiles number at most 24; some pairs in every draw have 24.
All inputs are finite; a program needn't handle non-finite values.
Results may differ from a plain program's by a relative error of at most 0.0055.
Values may be sent and summed in bfloat16 or wider, within the bound.
No kernel may reach another device: no remote copies, remote signals or barrier semaphores. Data moves between devices by JAX's collectives and lax.ppermute only.
A program may use at most 128 MiB of HBM per device.

v0:
```python
import math
import jax
import jax.numpy as jnp
from jax import lax
from jax.sharding import PartitionSpec as P


def xor_gather(data, axis_name, groups):
    count = lax.axis_size(axis_name)
    for group in groups:
        parts = [data]
        for code in range(1, 1 << len(group)):
            offset = sum((bit for k, bit in enumerate(group) if code >> k & 1))
            parts.append(lax.ppermute(data, axis_name, [(j, j ^ offset) for j in range(count)]))
        data = jnp.stack(parts)
    return data


def xor_parts(data, axis_name, group):
    count = lax.axis_size(axis_name)
    parts = [data]
    for code in range(1, 1 << len(group)):
        offset = sum((bit for k, bit in enumerate(group) if code >> k & 1))
        parts.append(lax.ppermute(data, axis_name, [(j, j ^ offset) for j in range(count)]))
    return parts


def stacked_position(offset, groups):
    position = jnp.zeros_like(offset)
    for group in reversed(groups):
        digit = sum((offset // bit % 2 << k for k, bit in enumerate(group)))
        position = position * (1 << len(group)) + digit
    return position


def bit_groups(bits):
    return [bits[k : k + 2] for k in range(0, len(bits), 2)]


def gather_operators(x_operator, y_operator, after):
    mem_count = lax.axis_size("mem")
    tile_count = lax.axis_size("tile")
    x_rows, x_cols = x_operator.shape
    y_rows, y_cols = y_operator.shape
    width = max(x_cols, y_cols)
    both = jnp.concatenate(
        [
            jnp.pad(x_operator, ((0, 0), (0, width - x_cols))),
            jnp.pad(y_operator, ((0, 0), (0, width - y_cols))),
        ]
    )
    mem_bits = bit_groups([1 << k for k in range(mem_count.bit_length() - 1)])
    tile_bits = bit_groups([1 << k for k in range(1, tile_count.bit_length() - 1)]) + [[1]]
    both = xor_gather(both, "mem", mem_bits)
    chip_groups = tile_bits[:-1]
    both = xor_gather(both, "tile", chip_groups[:-1])
    parts = xor_parts(both, "tile", chip_groups[-1]) if chip_groups else [both]
    parts, after = lax.optimization_barrier((parts, after))
    swapped = [
        lax.ppermute(part, "tile", [(j, j ^ 1) for j in range(tile_count)]) for part in parts
    ]
    both = jnp.stack([jnp.stack(parts), jnp.stack(swapped)])
    both = both.reshape(mem_count * tile_count, x_rows + y_rows, width)
    mem_of = lax.broadcasted_iota(jnp.int32, (mem_count, tile_count), 0)
    tile_of = lax.broadcasted_iota(jnp.int32, (mem_count, tile_count), 1)
    position = stacked_position(tile_of ^ lax.axis_index("tile"), tile_bits) * mem_count
    position = position + stacked_position(mem_of ^ lax.axis_index("mem"), mem_bits)
    position = position.reshape(-1)
    x_full = jnp.take(both[:, :x_rows, :x_cols], position, axis=0, mode="clip")
    y_full = jnp.take(both[:, x_rows:, :y_cols], position, axis=0, mode="clip")
    x_full = x_full.reshape(mem_count * tile_count * x_rows, x_cols)
    y_full = y_full.reshape(mem_count * tile_count * y_rows, y_cols)
    return (x_full, y_full, after)


def body(
    source_blocks, send_blocks, recv_slot, recv_weight, recv_count, regional, x_operator, y_operator
):
    tile_count = lax.axis_size("tile")
    member_count, level_count, columns, y_cells = regional.shape
    capacity = send_blocks.shape[2]
    block_cells = source_blocks.shape[3]
    block_side = math.isqrt(block_cells)
    picked = send_blocks[0].reshape(-1)
    held = source_blocks.shape[0]
    one_hot = (picked[:, None] == lax.broadcasted_iota(jnp.int32, (1, held), 1)).astype(
        source_blocks.dtype
    )
    packed = jnp.dot(
        one_hot, source_blocks.reshape(held, -1), preferred_element_type=jnp.float32
    ).astype(source_blocks.dtype)
    packed = packed.reshape(tile_count, capacity, -1)
    arrived = lax.all_to_all(packed, "tile", split_axis=0, concat_axis=0, tiled=True)
    slot_count = columns // block_side * (y_cells // block_side)
    live_mask = lax.broadcasted_iota(jnp.int32, (tile_count, capacity), 1) < recv_count[0][:, None]
    weights = jnp.where(live_mask, recv_weight[0], 0.0).reshape(-1)
    slot_match = recv_slot[0].reshape(-1)[None, :] == lax.broadcasted_iota(
        jnp.int32, (slot_count, tile_count * capacity), 0
    )
    remap_weights = jnp.where(slot_match, weights[None, :], 0.0).astype(jnp.bfloat16)
    remapped = jnp.dot(
        remap_weights,
        arrived.reshape(tile_count * capacity, -1),
        preferred_element_type=jnp.float32,
    )
    remapped = remapped.reshape(
        columns // block_side,
        y_cells // block_side,
        member_count,
        level_count,
        block_side,
        block_side,
    )
    remapped = remapped.transpose(2, 3, 0, 4, 1, 5).reshape(
        member_count, level_count, columns, y_cells
    )
    difference = (remapped - regional.astype(jnp.float32)).astype(jnp.bfloat16)
    x_full, y_full, difference = gather_operators(x_operator, y_operator, difference)
    x_lines = lax.all_to_all(difference, "tile", split_axis=3, concat_axis=2, tiled=True)
    after_first = jnp.einsum(
        "ax,mlxy->mlay", x_full, x_lines, preferred_element_type=jnp.float32
    ).astype(jnp.bfloat16)
    y_chunk = y_cells // tile_count
    outgoing = after_first.reshape(
        member_count, level_count, tile_count, columns, y_chunk
    ).transpose(2, 0, 1, 3, 4)
    tile_back = lax.all_to_all(outgoing, "tile", split_axis=0, concat_axis=0, tiled=True)
    after_second = jnp.einsum(
        "tmlxy,bty->mlxb",
        tile_back,
        y_full.reshape(y_cells, tile_count, y_chunk),
        preferred_element_type=jnp.float32,
    )
    return (regional.astype(jnp.float32) + after_second).astype(jnp.bfloat16)


def solution(mesh):
    placed = (
        P("tile", "mem", None, None),
        P("tile", None, None),
        P("tile", None, None),
        P("tile", None, None),
        P("tile", None),
        P("mem", None, "tile", None),
        P(("mem", "tile"), None),
        P(("mem", "tile"), None),
    )
    return jax.shard_map(
        body, mesh=mesh, in_specs=placed, out_specs=P("mem", None, "tile", None), check_vma=False
    )
```

profile of v0, /device:TPU:0, one launch (start us, length us, event | category | flops | bytes accessed | tf_op | source)
XLA Modules:
  0.0 54.1 jit_solution(3132020845288126406)
XLA Ops:
  0.0 0.8 %fusion.32 = (bf16[1,28,512]{2,1,0:T(8,128)(2,1)S(1)}, bf16[28,512]{1,0:T(8,128)(2,1)S(1)}) fusion(bf16[12,384]{1,0:T(8,128)(2,1)} %param.15, bf16[16,512]{1,0:T(8,128)(2,1)} %param.14), kind=kLoop, calls=%fused_computation.86 | loop fusion | flops 86016 | bytes 82944 | tf_op jit(solution)/shard_map/stack | solution.py:15
  0.8 3.0 %collective-permute-start = (bf16[28,512]{1,0:T(8,128)(2,1)S(1)}, bf16[28,512]{1,0:T(8,128)(2,1)S(1)}, u32[]{:S(2)}, u32[]{:S(2)}) collective-permute-start(bf16[28,512]{1,0:T(8,128)(2,1)S(1)} %get-tuple-element.16), channel_id=1, source_target_pairs={{0,8},{8,0},{16,24},{24,16},{1,9},{9,1},{17,25},{25,17},{2,10},{10... | collective-permute-start | bytes 86024 | tf_op jit(solution)/shard_map/ppermute | solution.py:14
  3.8 2.6 %collective-permute-start.1 = (bf16[28,512]{1,0:T(8,128)(2,1)S(1)}, bf16[28,512]{1,0:T(8,128)(2,1)S(1)}, u32[]{:S(2)}, u32[]{:S(2)}) collective-permute-start(bf16[28,512]{1,0:T(8,128)(2,1)S(1)} %get-tuple-element.16), channel_id=1, source_target_pairs={{0,16},{8,24},{16,0},{24,8},{1,17},{9,25},{17,1},{25,9},{2,18},{10... | collective-permute-start | bytes 86024 | tf_op jit(solution)/shard_map/ppermute | solution.py:14
  6.4 1.1 %reshape.467 = bf16[128,1024]{1,0:T(8,128)(2,1)S(1)} reshape(bf16[128,2,2,256]{3,2,1,0:T(2,128)(2,1)} %param.8) | data formatting | bytes 524288 | tf_op jit(solution)/shard_map/reshape | solution.py:90
  7.5 0.8 %eq.39 = s32[192]{0:T(256)S(1)} reshape(s32[1,8,24]{2,1,0:T(8,128)} %param.9) | data formatting | bytes 1536 | tf_op jit(solution)/shard_map/eq | solution.py:86
  8.3 1.1 %convolution_convert_fusion = bf16[192,1024]{1,0:T(8,128)(2,1)} fusion(bf16[128,1024]{1,0:T(8,128)(2,1)S(1)} %reshape.467, s32[192]{0:T(256)S(1)} %eq.39), kind=kOutput, calls=%fused_computation.3 | convolution fusion | flops 50552832 | bytes 656128 | tf_op jit(solution)/shard_map/dot_general | solution.py:89
  9.4 3.9 %all-to-all-start = ((bf16[8,24,1024]{2,1,0:T(8,128)(2,1)}), bf16[8,24,1024]{2,1,0:T(8,128)(2,1)S(1)}, u32[]{:S(2)}, u32[]{:S(2)}) async-start(bf16[8,24,1024]{2,1,0:T(8,128)(2,1)} %bitcast.7), calls=%async_computation | async-start | bytes 786432 | tf_op jit(solution)/shard_map/all_to_all | solution.py:93
  13.5 0.1 lt.42
  13.6 0.1 squeeze.3
  13.7 0.1 select_n.131
  13.8 0.1 select_n.128
  13.9 0.1 select_n.135
  14.0 0.1 iota.75
  14.2 0.1 iota.84
  14.3 0.1 eq.36
  14.4 0.7 %pad_maximum_fusion.1 = bf16[4,28,512]{2,1,0:T(8,128)(2,1)} fusion(bf16[1,28,512]{2,1,0:T(8,128)(2,1)S(1)} %bitcast.94, bf16[1,28,512]{2,1,0:T(8,128)(2,1)S(1)} %bitcast.93, bf16[1,28,512]{2,1,0:T(8,128)(2,1)S(1)} %bitcast.92, bf16[1,28,512]{2,1,0:T(8,128)(2,1)S(1)} %get-tuple-element.15), kind=kLoop, calls=%fused_computation.18 | loop fusion | flops 172032 | bytes 229376 | tf_op jit(solution)/shard_map/stack | solution.py:15
  15.1 2.0 %collective-permute-start.3 = (bf16[4,28,512]{2,1,0:T(8,128)(2,1)}, bf16[4,28,512]{2,1,0:T(8,128)(2,1)}, u32[]{:S(2)}, u32[]{:S(2)}) collective-permute-start(bf16[4,28,512]{2,1,0:T(8,128)(2,1)} %pad_maximum_fusion.1), channel_id=1, source_target_pairs={{0,2},{1,3},{2,0},{3,1},{4,6},{5,7},{6,4},{7,5},{8,10},{9,11},{10,... | collective-permute-start | bytes 344072 | tf_op jit(solution)/shard_map/ppermute | solution.py:24
  17.1 1.5 %collective-permute-start.4 = (bf16[4,28,512]{2,1,0:T(8,128)(2,1)}, bf16[4,28,512]{2,1,0:T(8,128)(2,1)}, u32[]{:S(2)}, u32[]{:S(2)}) collective-permute-start(bf16[4,28,512]{2,1,0:T(8,128)(2,1)} %pad_maximum_fusion.1), channel_id=1, source_target_pairs={{0,4},{1,5},{2,6},{3,7},{4,0},{5,1},{6,2},{7,3},{8,12},{9,13},{10,... | collective-permute-start | bytes 344072 | tf_op jit(solution)/shard_map/ppermute | solution.py:24
  18.6 3.5 %all-to-all-done = bf16[8,24,1024]{2,1,0:T(8,128)(2,1)S(1)} async-done(((bf16[8,24,1024]{2,1,0:T(8,128)(2,1)}), bf16[8,24,1024]{2,1,0:T(8,128)(2,1)S(1)}, u32[]{:S(2)}, u32[]{:S(2)}) %all-to-all-start) | async-done | bytes 393248 | tf_op jit(solution)/shard_map/all_to_all | solution.py:93
  22.1 0.2 copy.18
  22.3 1.9 %convolution_bitcast_fusion = f32[2,2,4,16,24,16]{4,5,3,1,0,2:T(8,128)} fusion(bf16[2,2,16,16,192,1]{4,3,2,1,0,5:T(8,128)(2,1)S(1)} %bitcast.81, bf16[192]{0:T(256)(128)(2,1)S(1)} %broadcast_select_fusion.3, s32[4,24]{1,0:T(4,128)S(1)} %multiply_add_fusion, s32[192]{0:T(256)S(1)} %eq.36), kind=kOutput, calls=%fused_computation.2 | convolution fusion | flops 37785600 | bytes 787968 | tf_op jit(solution)/shard_map/dot_general | solution.py:101
  24.2 2.2 %copy.19 = f32[2,2,4,16,24,16]{5,4,3,2,1,0:T(8,128)S(1)} copy(f32[2,2,4,16,24,16]{4,5,3,1,0,2:T(8,128)} %convolution_bitcast_fusion) | data formatting | bytes 786432 | tf_op jit(solution)/shard_map/transpose | solution.py:114
  26.4 0.9 %reshape.470 = f32[2,2,64,384]{3,2,1,0:T(8,128)S(1)} reshape(f32[2,2,4,16,24,16]{5,4,3,2,1,0:T(8,128)S(1)} %copy.19) | data formatting | bytes 786432 | tf_op jit(solution)/shard_map/reshape | solution.py:114
  27.3 1.0 %fusion.3 = bf16[2,2,64,384]{3,2,1,0:T(8,128)(2,1)S(1)} fusion(f32[2,2,64,384]{3,2,1,0:T(8,128)S(1)} %reshape.470, bf16[2,2,64,384]{3,2,1,0:T(8,128)(2,1)} %param.13), kind=kLoop, calls=%fused_computation.13 | loop fusion | flops 294912 | bytes 786432 | tf_op jit(solution)/shard_map/convert_element_type | solution.py:117
  28.4 0.5 collective-permute-start.7
  28.9 0.1 collective-permute-start.8
  29.0 0.4 collective-permute-start.9
  29.4 0.6 %copy.20 = bf16[2,2,64,384]{2,1,0,3:T(2,128)(2,1)S(1)} copy(bf16[2,2,64,384]{3,2,1,0:T(8,128)(2,1)S(1)} %fusion.3) | data formatting | bytes 393216 | tf_op jit(solution)/shard_map/optimization_barrier | solution.py:58
  30.0 1.0 %reshape.495 = bf16[8,2,6144]{2,1,0:T(2,128)(2,1)} reshape(bf16[384,2,2,64]{3,2,1,0:T(2,128)(2,1)S(1)} %bitcast.83) | data formatting | bytes 393216
  31.0 3.4 %all-to-all-start.1 = ((bf16[8,2,6144]{2,1,0:T(2,128)(2,1)}), bf16[8,2,6144]{2,1,0:T(2,128)(2,1)S(1)}, u32[]{:S(2)}, u32[]{:S(2)}) async-start(bf16[8,2,6144]{2,1,0:T(2,128)(2,1)} %reshape.495), calls=%async_computation.1 | async-start | bytes 393216 | tf_op jit(solution)/shard_map/all_to_all | solution.py:119
  34.4 1.2 %maximum_bitcast_fusion = bf16[1,4,4,28,512]{4,3,2,1,0:T(8,128)(2,1)S(1)} fusion(bf16[1,4,28,512]{3,2,1,0:T(8,128)(2,1)} %bitcast.19, bf16[1,4,28,512]{3,2,1,0:T(8,128)(2,1)} %bitcast.18, bf16[1,4,28,512]{3,2,1,0:T(8,128)(2,1)} %bitcast.17, bf16[1,4,28,512]{3,2,1,0:T(8,128)(2,1)} %bitcast.16), kind=kLoop, calls=%fused_computation.9 | loop fusion | flops 688128 | bytes 917504 | tf_op jit(solution)/shard_map/stack | solution.py:62
  35.6 0.1 maximum_bitcast_fusion.1
  35.7 0.1 pad_maximum_fusion
  35.8 0.6 %gather_fusion = bf16[32,16,512]{2,1,0:T(8,128)(2,1)S(1)} fusion(bf16[32,16,512]{2,1,0:T(8,128)(2,1)S(1)} %slice.12, s32[1024]{0:T(1024)S(1)} %pad_clamp_fusion), kind=kCustom, calls=%fused_computation | custom fusion | bytes 1048704 | tf_op jit(solution)/shard_map/jit(_take)/gather | solution.py:69
  36.4 4.1 %all-to-all-done.1 = bf16[8,2,6144]{2,1,0:T(2,128)(2,1)S(1)} async-done(((bf16[8,2,6144]{2,1,0:T(2,128)(2,1)}), bf16[8,2,6144]{2,1,0:T(2,128)(2,1)S(1)}, u32[]{:S(2)}, u32[]{:S(2)}) %all-to-all-start.1) | async-done | bytes 196640 | tf_op jit(solution)/shard_map/all_to_all | solution.py:119
  40.5 0.3 reshape.496
  40.8 0.3 copy.45
  41.1 0.3 all_to_all.23
  41.4 0.3 fusion
  41.7 0.2 reshape.473
  42.0 1.0 %reshape.497 = bf16[8,2,6144]{2,1,0:T(2,128)(2,1)} reshape(bf16[8,2,2,48,64]{4,3,2,1,0:T(8,128)(2,1)S(1)} %bitcast.86) | data formatting | bytes 393216
  43.0 3.4 %all-to-all-start.2 = ((bf16[8,2,6144]{2,1,0:T(2,128)(2,1)}), bf16[8,2,6144]{2,1,0:T(2,128)(2,1)S(1)}, u32[]{:S(2)}, u32[]{:S(2)}) async-start(bf16[8,2,6144]{2,1,0:T(2,128)(2,1)} %reshape.497), calls=%async_computation.2 | async-start | bytes 393216 | tf_op jit(solution)/shard_map/all_to_all | solution.py:127
  46.4 0.6 %gather_fusion.1 = bf16[32,12,384]{2,1,0:T(8,128)(2,1)S(1)} fusion(bf16[32,12,384]{2,1,0:T(8,128)(2,1)S(1)} %slice.13, s32[1024]{0:T(1024)S(1)} %pad_clamp_fusion), kind=kCustom, calls=%fused_computation.1 | custom fusion | bytes 589952 | tf_op jit(solution)/shard_map/jit(_take)/gather | solution.py:70
  47.1 0.7 %reshape_reshape.3 = bf16[384,8,48]{2,1,0:T(8,128)(2,1)S(1)} reshape(bf16[32,12,384]{2,1,0:T(8,128)(2,1)S(1)} %gather_fusion.1) | data formatting | bytes 589824 | tf_op jit(solution)/shard_map/reshape;reshape | solution.py:131
  47.8 4.8 %all-to-all-done.2 = bf16[8,2,6144]{2,1,0:T(2,128)(2,1)S(1)} async-done(((bf16[8,2,6144]{2,1,0:T(2,128)(2,1)}), bf16[8,2,6144]{2,1,0:T(2,128)(2,1)S(1)}, u32[]{:S(2)}, u32[]{:S(2)}) %all-to-all-start.2) | async-done | bytes 196640 | tf_op jit(solution)/shard_map/all_to_all | solution.py:127
  52.5 0.3 reshape.498
  52.8 0.5 fusion.1
  53.4 0.7 %fusion.4 = bf16[2,2,64,384]{3,2,1,0:T(8,128)(2,1)} fusion(bf16[2,2,64,384]{3,2,1,0:T(8,128)(2,1)S(1)} %copy-done, f32[2,2,64,384,1]{3,2,0,1,4:T(8,128)S(1)} %fusion.1), kind=kLoop, calls=%fused_computation.14 | loop fusion | flops 294912 | bytes 786432 | tf_op jit(solution)/shard_map/convert_element_type | solution.py:134
  (41 shorter events, 0.6 us)
Async XLA Ops:
  0.0 13.4 %copy-start.3 = (s32[1,8]{1,0:T(1,128)S(1)}, s32[1,8]{1,0:T(1,128)}, u32[]{:S(2)}) copy-start(s32[1,8]{1,0:T(1,128)} %param.12) | copy-start | bytes 100
  0.0 13.6 %copy-start.2 = (f32[1,8,24]{2,1,0:T(8,128)S(1)}, f32[1,8,24]{2,1,0:T(8,128)}, u32[]{:S(2)}) copy-start(f32[1,8,24]{2,1,0:T(8,128)} %param.11) | copy-start | bytes 2308
  0.0 14.3 %copy-start.1 = (s32[1,8,24]{2,1,0:T(8,128)S(1)}, s32[1,8,24]{2,1,0:T(8,128)}, u32[]{:S(2)}) copy-start(s32[1,8,24]{2,1,0:T(8,128)} %param.10) | copy-start | bytes 2308
  0.8 13.6 %collective-permute-start = (bf16[28,512]{1,0:T(8,128)(2,1)S(1)}, bf16[28,512]{1,0:T(8,128)(2,1)S(1)}, u32[]{:S(2)}, u32[]{:S(2)}) collective-permute-start(bf16[28,512]{1,0:T(8,128)(2,1)S(1)} %get-tuple-element.16), channel_id=1, source_target_pairs={{0,8},{8,0},{16,24},{24,16},{1,9},{9,1},{17,25},{25,17},{2,10},{10... | collective-permute-start | bytes 86024 | tf_op jit(solution)/shard_map/ppermute | solution.py:14
  3.8 10.6 %collective-permute-start.1 = (bf16[28,512]{1,0:T(8,128)(2,1)S(1)}, bf16[28,512]{1,0:T(8,128)(2,1)S(1)}, u32[]{:S(2)}, u32[]{:S(2)}) collective-permute-start(bf16[28,512]{1,0:T(8,128)(2,1)S(1)} %get-tuple-element.16), channel_id=1, source_target_pairs={{0,16},{8,24},{16,0},{24,8},{1,17},{9,25},{17,1},{25,9},{2,18},{10... | collective-permute-start | bytes 86024 | tf_op jit(solution)/shard_map/ppermute | solution.py:14
  6.4 8.0 %collective-permute-start.2 = (bf16[28,512]{1,0:T(8,128)(2,1)S(1)}, bf16[28,512]{1,0:T(8,128)(2,1)S(1)}, u32[]{:S(2)}, u32[]{:S(2)}) collective-permute-start(bf16[28,512]{1,0:T(8,128)(2,1)S(1)} %get-tuple-element.16), channel_id=1, source_target_pairs={{0,24},{8,16},{16,8},{24,0},{1,25},{9,17},{17,9},{25,1},{2,26},{10... | collective-permute-start | bytes 86024 | tf_op jit(solution)/shard_map/ppermute | solution.py:14
  9.4 12.8 %all-to-all-start = ((bf16[8,24,1024]{2,1,0:T(8,128)(2,1)}), bf16[8,24,1024]{2,1,0:T(8,128)(2,1)S(1)}, u32[]{:S(2)}, u32[]{:S(2)}) async-start(bf16[8,24,1024]{2,1,0:T(8,128)(2,1)} %bitcast.7), calls=%async_computation | async-start | bytes 786432 | tf_op jit(solution)/shard_map/all_to_all | solution.py:93
  15.1 13.2 %collective-permute-start.3 = (bf16[4,28,512]{2,1,0:T(8,128)(2,1)}, bf16[4,28,512]{2,1,0:T(8,128)(2,1)}, u32[]{:S(2)}, u32[]{:S(2)}) collective-permute-start(bf16[4,28,512]{2,1,0:T(8,128)(2,1)} %pad_maximum_fusion.1), channel_id=1, source_target_pairs={{0,2},{1,3},{2,0},{3,1},{4,6},{5,7},{6,4},{7,5},{8,10},{9,11},{10,... | collective-permute-start | bytes 344072 | tf_op jit(solution)/shard_map/ppermute | solution.py:24
  17.1 11.2 %collective-permute-start.4 = (bf16[4,28,512]{2,1,0:T(8,128)(2,1)}, bf16[4,28,512]{2,1,0:T(8,128)(2,1)}, u32[]{:S(2)}, u32[]{:S(2)}) collective-permute-start(bf16[4,28,512]{2,1,0:T(8,128)(2,1)} %pad_maximum_fusion.1), channel_id=1, source_target_pairs={{0,4},{1,5},{2,6},{3,7},{4,0},{5,1},{6,2},{7,3},{8,12},{9,13},{10,... | collective-permute-start | bytes 344072 | tf_op jit(solution)/shard_map/ppermute | solution.py:24
  18.6 9.7 %collective-permute-start.5 = (bf16[4,28,512]{2,1,0:T(8,128)(2,1)}, bf16[4,28,512]{2,1,0:T(8,128)(2,1)}, u32[]{:S(2)}, u32[]{:S(2)}) collective-permute-start(bf16[4,28,512]{2,1,0:T(8,128)(2,1)} %pad_maximum_fusion.1), channel_id=1, source_target_pairs={{0,6},{1,7},{2,4},{3,5},{4,2},{5,3},{6,0},{7,1},{8,14},{9,15},{10,... | collective-permute-start | bytes 344072 | tf_op jit(solution)/shard_map/ppermute | solution.py:24
  28.3 7.3 %collective-permute-start.6 = (bf16[4,28,512]{2,1,0:T(8,128)(2,1)}, bf16[4,28,512]{2,1,0:T(8,128)(2,1)S(1)}, u32[]{:S(2)}, u32[]{:S(2)}) collective-permute-start(bf16[4,28,512]{2,1,0:T(8,128)(2,1)} %pad_maximum_fusion.1), channel_id=1, source_target_pairs={{0,1},{1,0},{2,3},{3,2},{4,5},{5,4},{6,7},{7,6},{8,9},{9,8},{10,11... | collective-permute-start | bytes 344072 | tf_op jit(solution)/shard_map/ppermute | solution.py:60
  28.4 7.2 %collective-permute-start.7 = (bf16[4,28,512]{2,1,0:T(8,128)(2,1)}, bf16[4,28,512]{2,1,0:T(8,128)(2,1)S(1)}, u32[]{:S(2)}, u32[]{:S(2)}) collective-permute-start(bf16[4,28,512]{2,1,0:T(8,128)(2,1)} %collective-permute-done.3), channel_id=1, source_target_pairs={{0,1},{1,0},{2,3},{3,2},{4,5},{5,4},{6,7},{7,6},{8,9},{9,8},{10,11... | collective-permute-start | bytes 344072 | tf_op jit(solution)/shard_map/ppermute | solution.py:60
  28.9 6.7 %collective-permute-start.8 = (bf16[4,28,512]{2,1,0:T(8,128)(2,1)}, bf16[4,28,512]{2,1,0:T(8,128)(2,1)S(1)}, u32[]{:S(2)}, u32[]{:S(2)}) collective-permute-start(bf16[4,28,512]{2,1,0:T(8,128)(2,1)} %collective-permute-done.4), channel_id=1, source_target_pairs={{0,1},{1,0},{2,3},{3,2},{4,5},{5,4},{6,7},{7,6},{8,9},{9,8},{10,11... | collective-permute-start | bytes 344072 | tf_op jit(solution)/shard_map/ppermute | solution.py:60
  29.0 6.6 %collective-permute-start.9 = (bf16[4,28,512]{2,1,0:T(8,128)(2,1)}, bf16[4,28,512]{2,1,0:T(8,128)(2,1)S(1)}, u32[]{:S(2)}, u32[]{:S(2)}) collective-permute-start(bf16[4,28,512]{2,1,0:T(8,128)(2,1)} %collective-permute-done.5), channel_id=1, source_target_pairs={{0,1},{1,0},{2,3},{3,2},{4,5},{5,4},{6,7},{7,6},{8,9},{9,8},{10,11... | collective-permute-start | bytes 344072 | tf_op jit(solution)/shard_map/ppermute | solution.py:60
  31.0 9.6 %all-to-all-start.1 = ((bf16[8,2,6144]{2,1,0:T(2,128)(2,1)}), bf16[8,2,6144]{2,1,0:T(2,128)(2,1)S(1)}, u32[]{:S(2)}, u32[]{:S(2)}) async-start(bf16[8,2,6144]{2,1,0:T(2,128)(2,1)} %reshape.495), calls=%async_computation.1 | async-start | bytes 393216 | tf_op jit(solution)/shard_map/all_to_all | solution.py:119
  43.0 9.6 %all-to-all-start.2 = ((bf16[8,2,6144]{2,1,0:T(2,128)(2,1)}), bf16[8,2,6144]{2,1,0:T(2,128)(2,1)S(1)}, u32[]{:S(2)}, u32[]{:S(2)}) async-start(bf16[8,2,6144]{2,1,0:T(2,128)(2,1)} %reshape.497), calls=%async_computation.2 | async-start | bytes 393216 | tf_op jit(solution)/shard_map/all_to_all | solution.py:127
  46.4 6.9 %copy-start = (bf16[2,2,64,384]{3,2,1,0:T(8,128)(2,1)S(1)}, bf16[2,2,64,384]{3,2,1,0:T(8,128)(2,1)}, u32[]{:S(2)}) copy-start(bf16[2,2,64,384]{3,2,1,0:T(8,128)(2,1)} %param.13) | copy-start | bytes 589828
where the time goes:
time: 54.7 us; the launch traced here: 54.1 us
  starting transfers between devices  20.9 us (38%)
  waiting for transfers between devices  12.4 us (23%)
  local copies, waits for them, and re-layouts  11.9 us (22%)
  other arithmetic  4.78 us (9%)
  matrix products  3.76 us (7%)
    ppermute x3, starting transfers between devices, xor_gather(): lax.ppermute(data, axis_name, [(j, j ^ offset) for j in range(count)])  5.62 us
    all_to_all x1, waiting for transfers between devices, body(): lax.all_to_all(outgoing, 'tile', split_axis=0, concat_axis=0, tiled=True)  4.76 us
    all_to_all x1, waiting for transfers between devices, body(): lax.all_to_all(difference, 'tile', split_axis=3, concat_axis=2, tiled=True)  4.11 us
    all_to_all x1, starting transfers between devices, body(): lax.all_to_all(packed, 'tile', split_axis=0, concat_axis=0, tiled=True)  3.94 us
    all_to_all x1, waiting for transfers between devices, body(): lax.all_to_all(packed, 'tile', split_axis=0, concat_axis=0, tiled=True)  3.5 us
    ppermute x3, starting transfers between devices, xor_parts(): lax.ppermute(data, axis_name, [(j, j ^ offset) for j in range(count)])  3.49 us
    all_to_all x1, starting transfers between devices, body(): lax.all_to_all(difference, 'tile', split_axis=3, concat_axis=2, tiled=True)  3.39 us
    all_to_all x1, starting transfers between devices, body(): lax.all_to_all(outgoing, 'tile', split_axis=0, concat_axis=0, tiled=True)  3.39 us
  transfers between devices with their start and end apart: 13, of which 3 were waited for; matrix products, arithmetic and copies ran while one was open for 29% of the time, Pallas kernels for 0%

commit v1 on v0

--- a/solution.py
+++ b/solution.py
@@ -116,7 +116,9 @@
     )
     difference = (remapped - regional.astype(jnp.float32)).astype(jnp.bfloat16)
     x_full, y_full, difference = gather_operators(x_operator, y_operator, difference)
-    x_lines = lax.all_to_all(difference, "tile", split_axis=3, concat_axis=2, tiled=True)
+    pieces = jnp.split(difference, lax.axis_size("tile"), axis=3)
+    arrived_2 = lax.all_to_all(jnp.stack(pieces), "tile", 0, 0)
+    x_lines = jnp.concatenate(arrived_2, axis=2)
     after_first = jnp.einsum(
         "ax,mlxy->mlay", x_full, x_lines, preferred_element_type=jnp.float32
     ).astype(jnp.bfloat16)

time: 54.7 us -> 54 us (0.987)
  waiting for transfers between devices: 12.4 us -> 11.3 us
    all_to_all x1, waiting for transfers between devices: 4.11 us -> 2.86 us  [body(): arrived_2 = lax.all_to_all(jnp.stack(pieces), 'tile', 0, 0)]
    unnamed x12 -> x19, local copies, waits for them, and re-layouts: 2.56 us -> 3.18 us
    optimization_barrier x1 -> x0, local copies, waits for them, and re-layouts: 0.59 us -> none  [gather_operators(): parts, after = lax.optimization_barrier((parts, after))]
  transfers between devices with their start and end apart: 13 -> 13, of which waited for: 3 -> 4; matrix products, arithmetic and copies ran while one was open for 29% -> 26% of each run, Pallas kernels for 0% -> 0%
where the time goes in v1:
time: 54 us; the launch traced here: 53.4 us
  starting transfers between devices  20.9 us (39%)
  local copies, waits for them, and re-layouts  12.3 us (23%)
  waiting for transfers between devices  11.3 us (21%)
  other arithmetic  4.77 us (9%)
  matrix products  3.76 us (7%)
    ppermute x3, starting transfers between devices, xor_gather(): lax.ppermute(data, axis_name, [(j, j ^ offset) for j in range(count)])  5.62 us
    all_to_all x1, waiting for transfers between devices, body(): lax.all_to_all(outgoing, 'tile', split_axis=0, concat_axis=0, tiled=True)  4.76 us
    all_to_all x1, starting transfers between devices, body(): lax.all_to_all(packed, 'tile', split_axis=0, concat_axis=0, tiled=True)  3.94 us
    all_to_all x1, waiting for transfers between devices, body(): lax.all_to_all(packed, 'tile', split_axis=0, concat_axis=0, tiled=True)  3.5 us
    ppermute x3, starting transfers between devices, xor_parts(): lax.ppermute(data, axis_name, [(j, j ^ offset) for j in range(count)])  3.49 us
    all_to_all x1, starting transfers between devices, body(): arrived_2 = lax.all_to_all(jnp.stack(pieces), 'tile', 0, 0)  3.39 us
    all_to_all x1, starting transfers between devices, body(): lax.all_to_all(outgoing, 'tile', split_axis=0, concat_axis=0, tiled=True)  3.39 us
    unnamed x19, local copies, waits for them, and re-layouts  3.18 us
  transfers between devices with their start and end apart: 13, of which 4 were waited for; matrix products, arithmetic and copies ran while one was open for 26% of the time, Pallas kernels for 0%

profile of v1, /device:TPU:0, one launch (start us, length us, event | category | flops | bytes accessed | tf_op | source)
XLA Modules:
  0.0 53.4 jit_solution(7524736896458462390)
XLA Ops:
  0.0 0.8 %fusion.32 = (bf16[1,28,512]{2,1,0:T(8,128)(2,1)S(1)}, bf16[28,512]{1,0:T(8,128)(2,1)S(1)}) fusion(bf16[12,384]{1,0:T(8,128)(2,1)} %param.15, bf16[16,512]{1,0:T(8,128)(2,1)} %param.14), kind=kLoop, calls=%fused_computation.93 | loop fusion | flops 86016 | bytes 82944 | tf_op jit(solution)/shard_map/stack | solution.py:15
  0.8 3.0 %collective-permute-start = (bf16[28,512]{1,0:T(8,128)(2,1)S(1)}, bf16[28,512]{1,0:T(8,128)(2,1)S(1)}, u32[]{:S(2)}, u32[]{:S(2)}) collective-permute-start(bf16[28,512]{1,0:T(8,128)(2,1)S(1)} %get-tuple-element.16), channel_id=1, source_target_pairs={{0,8},{8,0},{16,24},{24,16},{1,9},{9,1},{17,25},{25,17},{2,10},{10... | collective-permute-start | bytes 86024 | tf_op jit(solution)/shard_map/ppermute | solution.py:14
  3.8 2.6 %collective-permute-start.1 = (bf16[28,512]{1,0:T(8,128)(2,1)S(1)}, bf16[28,512]{1,0:T(8,128)(2,1)S(1)}, u32[]{:S(2)}, u32[]{:S(2)}) collective-permute-start(bf16[28,512]{1,0:T(8,128)(2,1)S(1)} %get-tuple-element.16), channel_id=1, source_target_pairs={{0,16},{8,24},{16,0},{24,8},{1,17},{9,25},{17,1},{25,9},{2,18},{10... | collective-permute-start | bytes 86024 | tf_op jit(solution)/shard_map/ppermute | solution.py:14
  6.4 1.1 %reshape.473 = bf16[128,1024]{1,0:T(8,128)(2,1)S(1)} reshape(bf16[128,2,2,256]{3,2,1,0:T(2,128)(2,1)} %param.8) | data formatting | bytes 524288 | tf_op jit(solution)/shard_map/reshape | solution.py:90
  7.5 0.8 %eq.39 = s32[192]{0:T(256)S(1)} reshape(s32[1,8,24]{2,1,0:T(8,128)} %param.9) | data formatting | bytes 1536 | tf_op jit(solution)/shard_map/eq | solution.py:86
  8.3 1.1 %convolution_convert_fusion = bf16[192,1024]{1,0:T(8,128)(2,1)} fusion(bf16[128,1024]{1,0:T(8,128)(2,1)S(1)} %reshape.473, s32[192]{0:T(256)S(1)} %eq.39), kind=kOutput, calls=%fused_computation.3 | convolution fusion | flops 50552832 | bytes 656128 | tf_op jit(solution)/shard_map/dot_general | solution.py:89
  9.4 3.9 %all-to-all-start = ((bf16[8,24,1024]{2,1,0:T(8,128)(2,1)}), bf16[8,24,1024]{2,1,0:T(8,128)(2,1)S(1)}, u32[]{:S(2)}, u32[]{:S(2)}) async-start(bf16[8,24,1024]{2,1,0:T(8,128)(2,1)} %bitcast.7), calls=%async_computation | async-start | bytes 786432 | tf_op jit(solution)/shard_map/all_to_all | solution.py:93
  14.4 0.7 %pad_maximum_fusion.1 = bf16[4,28,512]{2,1,0:T(8,128)(2,1)} fusion(bf16[1,28,512]{2,1,0:T(8,128)(2,1)S(1)} %bitcast.106, bf16[1,28,512]{2,1,0:T(8,128)(2,1)S(1)} %bitcast.105, bf16[1,28,512]{2,1,0:T(8,128)(2,1)S(1)} %bitcast.104, bf16[1,28,512]{2,1,0:T(8,128)(2,1)S(1)} %get-tuple-element.15), kind=kLoop, calls=%fused_computation.17 | loop fusion | flops 172032 | bytes 229376 | tf_op jit(solution)/shard_map/stack | solution.py:15
  15.1 2.0 %collective-permute-start.3 = (bf16[4,28,512]{2,1,0:T(8,128)(2,1)}, bf16[4,28,512]{2,1,0:T(8,128)(2,1)}, u32[]{:S(2)}, u32[]{:S(2)}) collective-permute-start(bf16[4,28,512]{2,1,0:T(8,128)(2,1)} %pad_maximum_fusion.1), channel_id=1, source_target_pairs={{0,2},{1,3},{2,0},{3,1},{4,6},{5,7},{6,4},{7,5},{8,10},{9,11},{10,... | collective-permute-start | bytes 344072 | tf_op jit(solution)/shard_map/ppermute | solution.py:24
  17.1 1.5 %collective-permute-start.4 = (bf16[4,28,512]{2,1,0:T(8,128)(2,1)}, bf16[4,28,512]{2,1,0:T(8,128)(2,1)}, u32[]{:S(2)}, u32[]{:S(2)}) collective-permute-start(bf16[4,28,512]{2,1,0:T(8,128)(2,1)} %pad_maximum_fusion.1), channel_id=1, source_target_pairs={{0,4},{1,5},{2,6},{3,7},{4,0},{5,1},{6,2},{7,3},{8,12},{9,13},{10,... | collective-permute-start | bytes 344072 | tf_op jit(solution)/shard_map/ppermute | solution.py:24
  18.6 3.5 %all-to-all-done = bf16[8,24,1024]{2,1,0:T(8,128)(2,1)S(1)} async-done(((bf16[8,24,1024]{2,1,0:T(8,128)(2,1)}), bf16[8,24,1024]{2,1,0:T(8,128)(2,1)S(1)}, u32[]{:S(2)}, u32[]{:S(2)}) %all-to-all-start) | async-done | bytes 393248 | tf_op jit(solution)/shard_map/all_to_all | solution.py:93
  22.1 0.2 copy.18
  22.3 1.9 %convolution_bitcast_fusion = f32[2,2,4,16,24,16]{4,5,3,1,0,2:T(8,128)} fusion(bf16[2,2,16,16,192,1]{4,3,2,1,0,5:T(8,128)(2,1)S(1)} %bitcast.95, bf16[192]{0:T(256)(128)(2,1)S(1)} %broadcast_select_fusion.3, s32[4,24]{1,0:T(4,128)S(1)} %multiply_add_fusion, s32[192]{0:T(256)S(1)} %eq.36), kind=kOutput, calls=%fused_computation.2 | convolution fusion | flops 37785600 | bytes 787968 | tf_op jit(solution)/shard_map/dot_general | solution.py:101
  24.2 2.2 %copy.19 = f32[2,2,4,16,24,16]{5,4,3,2,1,0:T(8,128)S(1)} copy(f32[2,2,4,16,24,16]{4,5,3,1,0,2:T(8,128)} %convolution_bitcast_fusion) | data formatting | bytes 786432 | tf_op jit(solution)/shard_map/transpose | solution.py:114
  26.4 0.9 %reshape.476 = f32[2,2,64,384]{3,2,1,0:T(8,128)S(1)} reshape(f32[2,2,4,16,24,16]{5,4,3,2,1,0:T(8,128)S(1)} %copy.19) | data formatting | bytes 786432 | tf_op jit(solution)/shard_map/reshape | solution.py:114
  27.3 1.0 %fusion.3 = bf16[2,2,64,384]{3,2,1,0:T(8,128)(2,1)S(1)} fusion(f32[2,2,64,384]{3,2,1,0:T(8,128)S(1)} %reshape.476, bf16[2,2,64,384]{3,2,1,0:T(8,128)(2,1)} %param.13), kind=kLoop, calls=%fused_computation.13 | loop fusion | flops 294912 | bytes 786432 | tf_op jit(solution)/shard_map/convert_element_type | solution.py:117
  28.3 0.1 bitcast_dynamic-update-slice_fusion.6
  28.4 0.1 bitcast_dynamic-update-slice_fusion.5
  28.5 0.1 bitcast_dynamic-update-slice_fusion.4
  28.6 0.1 bitcast_dynamic-update-slice_fusion.3
  28.8 0.1 bitcast_dynamic-update-slice_fusion.2
  28.9 0.1 bitcast_dynamic-update-slice_fusion.1
  29.0 0.1 bitcast_dynamic-update-slice_fusion
  29.1 0.3 copy.20
  29.3 1.0 %reshape.503 = bf16[8,2,6144]{2,1,0:T(2,128)(2,1)} reshape(bf16[8,2,2,48,64]{4,3,2,1,0:T(8,128)(2,1)S(1)} %bitcast.97) | data formatting | bytes 393216
  30.3 3.4 %all-to-all-start.1 = ((bf16[8,2,6144]{2,1,0:T(2,128)(2,1)}), bf16[8,2,6144]{2,1,0:T(2,128)(2,1)S(1)}, u32[]{:S(2)}, u32[]{:S(2)}) async-start(bf16[8,2,6144]{2,1,0:T(2,128)(2,1)} %reshape.503), calls=%async_computation.1 | async-start | bytes 393216 | tf_op jit(solution)/shard_map/all_to_all | solution.py:120
  33.7 0.4 collective-permute-start.6
  34.1 0.2 collective-permute-start.7
  34.3 0.3 collective-permute-start.8
  34.6 0.2 collective-permute-start.9
  34.8 1.2 %maximum_bitcast_fusion = bf16[1,4,4,28,512]{4,3,2,1,0:T(8,128)(2,1)S(1)} fusion(bf16[1,4,28,512]{3,2,1,0:T(8,128)(2,1)} %bitcast.25, bf16[1,4,28,512]{3,2,1,0:T(8,128)(2,1)} %bitcast.24, bf16[1,4,28,512]{3,2,1,0:T(8,128)(2,1)} %bitcast.23, bf16[1,4,28,512]{3,2,1,0:T(8,128)(2,1)} %bitcast.22), kind=kLoop, calls=%fused_computation.9 | loop fusion | flops 688128 | bytes 917504 | tf_op jit(solution)/shard_map/stack | solution.py:62
  36.0 0.2 collective-permute-done.9
  36.3 0.1 pad_maximum_fusion
  36.4 0.6 %gather_fusion = bf16[32,16,512]{2,1,0:T(8,128)(2,1)S(1)} fusion(bf16[32,16,512]{2,1,0:T(8,128)(2,1)S(1)} %slice.12, s32[1024]{0:T(1024)S(1)} %pad_clamp_fusion), kind=kCustom, calls=%fused_computation | custom fusion | bytes 1048704 | tf_op jit(solution)/shard_map/jit(_take)/gather | solution.py:69
  37.0 2.9 %all-to-all-done.1 = bf16[8,2,6144]{2,1,0:T(2,128)(2,1)S(1)} async-done(((bf16[8,2,6144]{2,1,0:T(2,128)(2,1)}), bf16[8,2,6144]{2,1,0:T(2,128)(2,1)S(1)}, u32[]{:S(2)}, u32[]{:S(2)}) %all-to-all-start.1) | async-done | bytes 196640 | tf_op jit(solution)/shard_map/all_to_all | solution.py:120
  39.9 0.3 reshape.504
  40.2 0.3 copy.21
  40.5 0.3 reshape.478
  40.7 0.3 fusion
  41.1 0.2 reshape.481
  41.4 1.0 %reshape.505 = bf16[8,2,6144]{2,1,0:T(2,128)(2,1)} reshape(bf16[8,2,2,48,64]{4,3,2,1,0:T(8,128)(2,1)S(1)} %bitcast.98) | data formatting | bytes 393216
  42.3 3.4 %all-to-all-start.2 = ((bf16[8,2,6144]{2,1,0:T(2,128)(2,1)}), bf16[8,2,6144]{2,1,0:T(2,128)(2,1)S(1)}, u32[]{:S(2)}, u32[]{:S(2)}) async-start(bf16[8,2,6144]{2,1,0:T(2,128)(2,1)} %reshape.505), calls=%async_computation.2 | async-start | bytes 393216 | tf_op jit(solution)/shard_map/all_to_all | solution.py:129
  45.8 0.6 %gather_fusion.1 = bf16[32,12,384]{2,1,0:T(8,128)(2,1)S(1)} fusion(bf16[32,12,384]{2,1,0:T(8,128)(2,1)S(1)} %slice.13, s32[1024]{0:T(1024)S(1)} %pad_clamp_fusion), kind=kCustom, calls=%fused_computation.1 | custom fusion | bytes 589952 | tf_op jit(solution)/shard_map/jit(_take)/gather | solution.py:70
  46.4 0.7 %reshape_reshape.3 = bf16[384,8,48]{2,1,0:T(8,128)(2,1)S(1)} reshape(bf16[32,12,384]{2,1,0:T(8,128)(2,1)S(1)} %gather_fusion.1) | data formatting | bytes 589824 | tf_op jit(solution)/shard_map/reshape;reshape | solution.py:133
  47.1 4.8 %all-to-all-done.2 = bf16[8,2,6144]{2,1,0:T(2,128)(2,1)S(1)} async-done(((bf16[8,2,6144]{2,1,0:T(2,128)(2,1)}), bf16[8,2,6144]{2,1,0:T(2,128)(2,1)S(1)}, u32[]{:S(2)}, u32[]{:S(2)}) %all-to-all-start.2) | async-done | bytes 196640 | tf_op jit(solution)/shard_map/all_to_all | solution.py:129
  51.9 0.3 reshape.506
  52.2 0.5 fusion.1
  52.7 0.7 %fusion.4 = bf16[2,2,64,384]{3,2,1,0:T(8,128)(2,1)} fusion(bf16[2,2,64,384]{3,2,1,0:T(8,128)(2,1)S(1)} %copy-done, f32[2,2,64,384,1]{3,2,0,1,4:T(8,128)S(1)} %fusion.1), kind=kLoop, calls=%fused_computation.14 | loop fusion | flops 294912 | bytes 786432 | tf_op jit(solution)/shard_map/convert_element_type | solution.py:136
  (50 shorter events, 1.3 us)
Async XLA Ops:
  0.0 13.4 %copy-start.3 = (s32[1,8]{1,0:T(1,128)S(1)}, s32[1,8]{1,0:T(1,128)}, u32[]{:S(2)}) copy-start(s32[1,8]{1,0:T(1,128)} %param.12) | copy-start | bytes 100
  0.0 13.6 %copy-start.2 = (f32[1,8,24]{2,1,0:T(8,128)S(1)}, f32[1,8,24]{2,1,0:T(8,128)}, u32[]{:S(2)}) copy-start(f32[1,8,24]{2,1,0:T(8,128)} %param.11) | copy-start | bytes 2308
  0.0 14.3 %copy-start.1 = (s32[1,8,24]{2,1,0:T(8,128)S(1)}, s32[1,8,24]{2,1,0:T(8,128)}, u32[]{:S(2)}) copy-start(s32[1,8,24]{2,1,0:T(8,128)} %param.10) | copy-start | bytes 2308
  0.8 13.6 %collective-permute-start = (bf16[28,512]{1,0:T(8,128)(2,1)S(1)}, bf16[28,512]{1,0:T(8,128)(2,1)S(1)}, u32[]{:S(2)}, u32[]{:S(2)}) collective-permute-start(bf16[28,512]{1,0:T(8,128)(2,1)S(1)} %get-tuple-element.16), channel_id=1, source_target_pairs={{0,8},{8,0},{16,24},{24,16},{1,9},{9,1},{17,25},{25,17},{2,10},{10... | collective-permute-start | bytes 86024 | tf_op jit(solution)/shard_map/ppermute | solution.py:14
  3.8 10.6 %collective-permute-start.1 = (bf16[28,512]{1,0:T(8,128)(2,1)S(1)}, bf16[28,512]{1,0:T(8,128)(2,1)S(1)}, u32[]{:S(2)}, u32[]{:S(2)}) collective-permute-start(bf16[28,512]{1,0:T(8,128)(2,1)S(1)} %get-tuple-element.16), channel_id=1, source_target_pairs={{0,16},{8,24},{16,0},{24,8},{1,17},{9,25},{17,1},{25,9},{2,18},{10... | collective-permute-start | bytes 86024 | tf_op jit(solution)/shard_map/ppermute | solution.py:14
  6.4 8.0 %collective-permute-start.2 = (bf16[28,512]{1,0:T(8,128)(2,1)S(1)}, bf16[28,512]{1,0:T(8,128)(2,1)S(1)}, u32[]{:S(2)}, u32[]{:S(2)}) collective-permute-start(bf16[28,512]{1,0:T(8,128)(2,1)S(1)} %get-tuple-element.16), channel_id=1, source_target_pairs={{0,24},{8,16},{16,8},{24,0},{1,25},{9,17},{17,9},{25,1},{2,26},{10... | collective-permute-start | bytes 86024 | tf_op jit(solution)/shard_map/ppermute | solution.py:14
  9.4 12.8 %all-to-all-start = ((bf16[8,24,1024]{2,1,0:T(8,128)(2,1)}), bf16[8,24,1024]{2,1,0:T(8,128)(2,1)S(1)}, u32[]{:S(2)}, u32[]{:S(2)}) async-start(bf16[8,24,1024]{2,1,0:T(8,128)(2,1)} %bitcast.7), calls=%async_computation | async-start | bytes 786432 | tf_op jit(solution)/shard_map/all_to_all | solution.py:93
  15.1 13.2 %collective-permute-start.3 = (bf16[4,28,512]{2,1,0:T(8,128)(2,1)}, bf16[4,28,512]{2,1,0:T(8,128)(2,1)}, u32[]{:S(2)}, u32[]{:S(2)}) collective-permute-start(bf16[4,28,512]{2,1,0:T(8,128)(2,1)} %pad_maximum_fusion.1), channel_id=1, source_target_pairs={{0,2},{1,3},{2,0},{3,1},{4,6},{5,7},{6,4},{7,5},{8,10},{9,11},{10,... | collective-permute-start | bytes 344072 | tf_op jit(solution)/shard_map/ppermute | solution.py:24
  17.1 11.2 %collective-permute-start.4 = (bf16[4,28,512]{2,1,0:T(8,128)(2,1)}, bf16[4,28,512]{2,1,0:T(8,128)(2,1)}, u32[]{:S(2)}, u32[]{:S(2)}) collective-permute-start(bf16[4,28,512]{2,1,0:T(8,128)(2,1)} %pad_maximum_fusion.1), channel_id=1, source_target_pairs={{0,4},{1,5},{2,6},{3,7},{4,0},{5,1},{6,2},{7,3},{8,12},{9,13},{10,... | collective-permute-start | bytes 344072 | tf_op jit(solution)/shard_map/ppermute | solution.py:24
  18.6 9.7 %collective-permute-start.5 = (bf16[4,28,512]{2,1,0:T(8,128)(2,1)}, bf16[4,28,512]{2,1,0:T(8,128)(2,1)}, u32[]{:S(2)}, u32[]{:S(2)}) collective-permute-start(bf16[4,28,512]{2,1,0:T(8,128)(2,1)} %pad_maximum_fusion.1), channel_id=1, source_target_pairs={{0,6},{1,7},{2,4},{3,5},{4,2},{5,3},{6,0},{7,1},{8,14},{9,15},{10,... | collective-permute-start | bytes 344072 | tf_op jit(solution)/shard_map/ppermute | solution.py:24
  30.3 9.6 %all-to-all-start.1 = ((bf16[8,2,6144]{2,1,0:T(2,128)(2,1)}), bf16[8,2,6144]{2,1,0:T(2,128)(2,1)S(1)}, u32[]{:S(2)}, u32[]{:S(2)}) async-start(bf16[8,2,6144]{2,1,0:T(2,128)(2,1)} %reshape.503), calls=%async_computation.1 | async-start | bytes 393216 | tf_op jit(solution)/shard_map/all_to_all | solution.py:120
  33.7 2.3 %collective-permute-start.6 = (bf16[4,28,512]{2,1,0:T(8,128)(2,1)}, bf16[4,28,512]{2,1,0:T(8,128)(2,1)S(1)}, u32[]{:S(2)}, u32[]{:S(2)}) collective-permute-start(bf16[4,28,512]{2,1,0:T(8,128)(2,1)} %pad_maximum_fusion.1), channel_id=1, source_target_pairs={{0,1},{1,0},{2,3},{3,2},{4,5},{5,4},{6,7},{7,6},{8,9},{9,8},{10,11... | collective-permute-start | bytes 344072 | tf_op jit(solution)/shard_map/ppermute | solution.py:60
  34.1 1.9 %collective-permute-start.7 = (bf16[4,28,512]{2,1,0:T(8,128)(2,1)}, bf16[4,28,512]{2,1,0:T(8,128)(2,1)S(1)}, u32[]{:S(2)}, u32[]{:S(2)}) collective-permute-start(bf16[4,28,512]{2,1,0:T(8,128)(2,1)} %collective-permute-done.3), channel_id=1, source_target_pairs={{0,1},{1,0},{2,3},{3,2},{4,5},{5,4},{6,7},{7,6},{8,9},{9,8},{10,11... | collective-permute-start | bytes 344072 | tf_op jit(solution)/shard_map/ppermute | solution.py:60
  34.3 1.7 %collective-permute-start.8 = (bf16[4,28,512]{2,1,0:T(8,128)(2,1)}, bf16[4,28,512]{2,1,0:T(8,128)(2,1)S(1)}, u32[]{:S(2)}, u32[]{:S(2)}) collective-permute-start(bf16[4,28,512]{2,1,0:T(8,128)(2,1)} %collective-permute-done.4), channel_id=1, source_target_pairs={{0,1},{1,0},{2,3},{3,2},{4,5},{5,4},{6,7},{7,6},{8,9},{9,8},{10,11... | collective-permute-start | bytes 344072 | tf_op jit(solution)/shard_map/ppermute | solution.py:60
  34.6 1.6 %collective-permute-start.9 = (bf16[4,28,512]{2,1,0:T(8,128)(2,1)}, bf16[4,28,512]{2,1,0:T(8,128)(2,1)S(1)}, u32[]{:S(2)}, u32[]{:S(2)}) collective-permute-start(bf16[4,28,512]{2,1,0:T(8,128)(2,1)} %collective-permute-done.5), channel_id=1, source_target_pairs={{0,1},{1,0},{2,3},{3,2},{4,5},{5,4},{6,7},{7,6},{8,9},{9,8},{10,11... | collective-permute-start | bytes 344072 | tf_op jit(solution)/shard_map/ppermute | solution.py:60
  42.3 9.6 %all-to-all-start.2 = ((bf16[8,2,6144]{2,1,0:T(2,128)(2,1)}), bf16[8,2,6144]{2,1,0:T(2,128)(2,1)S(1)}, u32[]{:S(2)}, u32[]{:S(2)}) async-start(bf16[8,2,6144]{2,1,0:T(2,128)(2,1)} %reshape.505), calls=%async_computation.2 | async-start | bytes 393216 | tf_op jit(solution)/shard_map/all_to_all | solution.py:129
  45.8 6.9 %copy-start = (bf16[2,2,64,384]{3,2,1,0:T(8,128)(2,1)S(1)}, bf16[2,2,64,384]{3,2,1,0:T(8,128)(2,1)}, u32[]{:S(2)}) copy-start(bf16[2,2,64,384]{3,2,1,0:T(8,128)(2,1)} %param.13) | copy-start | bytes 589828
